TPU v7x, 256 devices: a whole 4x4x8 slice. The times are simulated.
256 devices in a mesh: expert: 8 (over x, core), tensor: 32 (over z, y).
Axes of the slice: x: 4, y: 4, z: 8, core: 2. Of those that a mesh axis runs over, the one named last changes fastest.
Arguments:
- resid: bfloat16 [16384, 2048], P(('expert', 'tensor')), may hold values from -6 to 6
- contexts: bfloat16 [16384, 4096], P('expert', 'tensor'), may hold values from -6 to 6
- att_routes: int32 [16384, 2], P('expert'), may hold values from 0 to 7, all different within a row
- att_scores: float32 [16384, 2], P('expert'), may hold values from -6 to 6
- att_out_w: bfloat16 [8, 2048, 2048], P(None, 'tensor'), may hold values from -0.125 to 0.125
- norm_gain: bfloat16 [2048], replicated, may hold values from 0.25 to 1.75
- router_w: bfloat16 [2048, 8], replicated, may hold values from -0.125 to 0.125
- mlp_routes: int32 [16384, 2], P(('expert', 'tensor')), may hold values from 0 to 7, all different within a row
- split_rule: int32 [16384, 2], P(('expert', 'tensor')), may hold values from 0 to 2519
- placement: int32 [32], replicated, may hold values from 0 to 7, as said below
- cap_blocks: int32 [32], replicated, may hold values from 1 to 2, as said below
- w_gate_up: bfloat16 [32, 2048, 2, 5632], P('tensor', None, None, 'expert'), as said below
- w_down: bfloat16 [32, 5632, 2048], P('tensor', 'expert'), as said below
- final_gain: bfloat16 [2048], replicated, may hold values from 0.25 to 1.75
Outputs:
- stream_out: bfloat16 [16384, 2048], P(('expert', 'tensor'))
- normalized: bfloat16 [16384, 2048], P(('expert', 'tensor'))
Inputs may be any that keep to these rules, and one draw needn't show every extreme that they name: `att_routes`: each row names 2 different experts. `mlp_routes`: each row names 2 different experts. `placement`: every expert is held by at least one slot. `cap_blocks`: some slot accepts 2 blocks. `w_gate_up`: slots that hold the same expert hold equal weights. `w_down`: slots that hold the same expert hold equal weights.
All inputs are finite; a program needn't handle non-finite values.
Results may differ from a plain program's by a relative error of at most 0.023.
Values may be sent and summed in bfloat16 or wider, within the bound.
No kernel may reach another device: no remote copies, remote signals or barrier semaphores. Data moves between devices by JAX's collectives and lax.ppermute only.
A program may use at most 64 MiB of HBM per device.

v0:
```python
import jax
import jax.numpy as jnp
from jax import lax
from jax.sharding import PartitionSpec as P

MAXB = 2
norm_eps = 1e-06


def rms_norm(values, gain):
    scale = lax.rsqrt(jnp.mean(values * values, axis=-1, keepdims=True) + norm_eps)
    return values * scale * gain.astype(values.dtype)


def pair_gates(scores):
    first = jax.nn.silu(scores[:, 0:1] * 0.0) * 0.0 + jax.nn.sigmoid(
        scores[:, 0:1] - scores[:, 1:2]
    )
    first = first[:, 0]
    return jnp.stack([first, 1.0 - first], axis=1)


def activate(shard_piece, w_gate_up):
    both = jnp.einsum(
        "tsecd,sdgf->tsecgf", shard_piece, w_gate_up, preferred_element_type=jnp.float32
    )
    hidden = (jax.nn.silu(both[:, :, :, :, 0, :]) * both[:, :, :, :, 1, :]).astype(jnp.bfloat16)
    hidden = jnp.transpose(hidden, (0, 2, 3, 1, 4))
    return hidden.reshape(
        hidden.shape[0] * hidden.shape[1] * hidden.shape[2], hidden.shape[3], hidden.shape[4]
    )


def per_device(
    resid,
    contexts,
    att_routes,
    att_scores,
    att_out_w,
    norm_gain,
    router_w,
    mlp_routes,
    split_rule,
    placement,
    cap_blocks,
    w_gate_up,
    w_down,
    final_gain,
):
    n_tensor = lax.axis_size("tensor")
    row_count = resid.shape[0]
    model_width = resid.shape[1]
    group_rows = contexts.shape[0]
    att_experts = att_out_w.shape[0]
    slice_ctx = att_out_w.shape[1]
    top_count = att_routes.shape[1]
    gate_att = pair_gates(att_scores)
    chosen = (
        att_routes[:, :, None] == jnp.arange(att_experts, dtype=jnp.int32)[None, None, :]
    ).astype(jnp.float32)
    weighted = chosen * gate_att[:, :, None]
    context_part = contexts.reshape(group_rows, slice_ctx, top_count).astype(jnp.float32)
    mixed = (
        jnp.einsum("tke,tck->tec", weighted, context_part)
        .astype(jnp.bfloat16)
        .reshape(group_rows, att_experts * slice_ctx)
    )
    weight_flat = att_out_w.reshape(att_experts * slice_ctx, model_width)
    row_block = mixed
    attention = lax.psum_scatter(
        jnp.dot(row_block, weight_flat, preferred_element_type=jnp.float32).astype(jnp.bfloat16),
        "tensor",
        scatter_dimension=0,
        tiled=True,
    ).astype(jnp.float32)
    stream = (resid.astype(jnp.float32) + attention).astype(jnp.bfloat16)
    normed = rms_norm(stream.astype(jnp.float32), norm_gain).astype(jnp.bfloat16)
    logits = jnp.dot(normed, router_w, preferred_element_type=jnp.float32)
    gate_mlp = pair_gates(jnp.take_along_axis(logits, mlp_routes, axis=1))
    replicas = placement.shape[0]
    slots = w_gate_up.shape[0]
    expert_total = router_w.shape[1]
    block_rows = max(1, row_count * top_count // (2 * replicas))
    capacity_rows = MAXB * block_rows
    slot_ids = jnp.arange(replicas, dtype=jnp.int32)
    expert_ids = jnp.arange(expert_total, dtype=jnp.int32)
    copies = jnp.sum((placement[None, :] == expert_ids[:, None]).astype(jnp.int32), axis=1)
    earlier = jnp.sum(
        (
            (placement[None, :] == placement[:, None]) & (slot_ids[None, :] < slot_ids[:, None])
        ).astype(jnp.int32),
        axis=1,
    )
    route_onehot = (mlp_routes[:, :, None] == expert_ids[None, None, :]).astype(jnp.int32)
    route_copies = jnp.sum(route_onehot * copies[None, None, :], axis=2)
    replica_rank = jnp.remainder(split_rule, route_copies)
    match = (
        (placement[None, None, :] == mlp_routes[:, :, None])
        & (earlier[None, None, :] == replica_rank[:, :, None])
    ).astype(jnp.int32)
    replica_slot = jnp.sum(match * slot_ids[None, None, :], axis=2)
    capacity = jnp.sum(match * cap_blocks[None, None, :], axis=2) * block_rows
    flat_match = match.reshape(row_count * top_count, replicas)
    before = jnp.cumsum(flat_match, axis=0) - flat_match
    arrival = jnp.sum(before * flat_match, axis=1).reshape(row_count, top_count)
    is_kept = arrival < capacity
    holder = replica_slot // slots
    within = replica_slot % slots
    position = within * (n_tensor * capacity_rows) + holder * capacity_rows + arrival
    position = jnp.where(is_kept, position, -1)
    buffer_rows = slots * n_tensor * capacity_rows
    placer = jnp.sum(
        (jnp.arange(buffer_rows, dtype=jnp.int32)[:, None, None] == position[None, :, :]).astype(
            jnp.bfloat16
        ),
        axis=2,
    )
    send_rows = jnp.dot(placer, normed, preferred_element_type=jnp.float32).astype(jnp.bfloat16)
    send_rows = send_rows.reshape(slots, n_tensor, capacity_rows, model_width)
    collected = lax.all_gather(send_rows[None], "expert", axis=0, tiled=True)
    arrived = lax.all_to_all(collected, "tensor", split_axis=2, concat_axis=2, tiled=True)
    hidden = activate(arrived, w_gate_up)
    row_block = hidden
    summed = lax.psum_scatter(
        jnp.einsum("bsf,sfd->bsd", row_block, w_down, preferred_element_type=jnp.float32).astype(
            jnp.bfloat16
        ),
        "expert",
        scatter_dimension=0,
        tiled=True,
    )
    results = summed.reshape(n_tensor, capacity_rows, slots, model_width)
    returned = lax.all_to_all(results, "tensor", split_axis=0, concat_axis=0, tiled=True)
    flat_back = returned.reshape(n_tensor * capacity_rows * slots, model_width)
    back_index = jnp.where(is_kept, holder * (capacity_rows * slots) + arrival * slots + within, 0)
    fetched = (
        jnp.take(flat_back, back_index.reshape(-1), axis=0)
        .reshape(row_count, top_count, model_width)
        .astype(jnp.float32)
    )
    factors = gate_mlp * is_kept.astype(jnp.float32)
    expert_mix = fetched[:, 0, :] * factors[:, 0:1] + fetched[:, 1, :] * factors[:, 1:2]
    after = stream.astype(jnp.float32) + expert_mix
    return (after.astype(jnp.bfloat16), rms_norm(after, final_gain).astype(jnp.bfloat16))


def solution(mesh):
    return jax.shard_map(
        per_device,
        mesh=mesh,
        in_specs=(
            P(("expert", "tensor"), None),
            P("expert", "tensor"),
            P("expert", None),
            P("expert", None),
            P(None, "tensor", None),
            P(),
            P(),
            P(("expert", "tensor"), None),
            P(("expert", "tensor"), None),
            P(),
            P(),
            P("tensor", None, None, "expert"),
            P("tensor", "expert", None),
            P(),
        ),
        out_specs=(P(("expert", "tensor"), None), P(("expert", "tensor"), None)),
        check_vma=False,
    )
```

profile of v0, /device:TPU:7, one launch (start us, length us, event | category | flops | bytes accessed | tf_op | source)
XLA Modules:
  0.0 516.6 jit_solution(11836133515749787276)
XLA Ops:
  7.2 2.2 copy.77
  9.4 1.4 reshape.175
  10.8 2.1 copy.78
  13.0 0.3 copy.76
  13.3 1.4 copy.75
  14.7 14.3 %convolution_convert_fusion = bf16[2048,8,64]{2,1,0:T(8,128)(2,1)S(1)} fusion(bf16[2048,64,2]{1,2,0:T(2,128)(2,1)} %copy.78, bf16[2048,2]{1,0:T(8,128)(2,1)S(1)} %copy.76, s32[2048,2]{1,0:T(8,128)} %copy.75), kind=kOutput, calls=%fused_computation.14 | convolution fusion | flops 4259840 | bytes 2646016 | tf_op jit(solution)/shard_map/tke,tck->tec/dot_general | solution.py:64
  29.0 7.0 %bitcast_convert_fusion = bf16[2048,2048]{1,0:T(8,128)(2,1)} fusion(bf16[8,64,2048]{2,1,0:T(8,128)(2,1)S(1)} %copy-done.11, bf16[2048,8,64]{2,1,0:T(8,128)(2,1)S(1)} %convolution_convert_fusion), kind=kOutput, calls=%fused_computation.2 | convolution fusion | flops 4299161600 | bytes 12582912 | tf_op jit(solution)/shard_map/dot_general | solution.py:71
  36.1 0.6 copy-done.7
  36.7 0.1 convert_reduce_fusion.1
  36.9 0.1 and_select_fusion.1
  37.1 0.1 copy.81
  37.2 0.1 eq.133
  37.3 0.1 eq.119
  37.5 0.2 convert_reduce_fusion
  37.6 0.1 fusion.27
  37.7 0.2 reduce_window_sum.11
  37.9 0.2 select_reduce_fusion
  38.1 0.1 reduce_sum.92
  38.3 0.1 select_reduce_fusion.2
  38.5 225.3 %reduce-scatter.3.cloned.1.call-done = bf16[64,2048]{1,0:T(8,128)(2,1)} async-done(((bf16[2048,2048]{1,0:T(8,128)(2,1)}), bf16[64,2048]{1,0:T(8,128)(2,1)}) %reduce-scatter.3.cloned.1.call-update) | async-done | bytes 262160 | tf_op jit(solution)/shard_map/reduce_scatter | solution.py:70
  263.9 1.1 fusion.16
  265.0 1.2 convolution_convert_fusion.1
  266.2 2.0 broadcast_in_dim_reshape.3
  268.2 2.1 copy.84
  270.4 35.7 %all-gather.2.cloned.1.call-done = bf16[8,1,32,4,2048]{4,2,3,1,0:T(8,128)(2,1)} async-done(((bf16[1,1,32,4,2048]{4,2,3,1,0:T(8,128)(2,1)}), bf16[8,1,32,4,2048]{4,2,3,1,0:T(8,128)(2,1)}) %all-gather.2.cloned.1.call-update) | async-done | bytes 4194320 | tf_op jit(solution)/shard_map/all_gather | solution.py:120
  306.1 5.6 %copy.85 = bf16[8,1,32,4,2048]{4,3,0,1,2:T(4,128)(2,1)S(1)} copy(bf16[8,1,32,4,2048]{4,2,3,1,0:T(8,128)(2,1)} %all-gather.2.cloned.1.call-done) | data formatting | bytes 8388608 | tf_op jit(solution)/shard_map/all_gather | solution.py:120
  311.7 103.9 %all_to_all.10 = bf16[8,1,32,4,2048]{4,3,0,1,2:T(4,128)(2,1)S(1)} all-to-all(bf16[8,1,32,4,2048]{4,3,0,1,2:T(4,128)(2,1)S(1)} %copy.85), channel_id=1, replica_groups=mesh['expert'=8,'tensor'=32] {'tensor'}, dimensions={2} | all-to-all | bytes 8388608 | tf_op jit(solution)/shard_map/all_to_all | solution.py:121
  415.7 7.3 %fusion.7 = f32[8,1,32,4,2,704]{5,2,4,3,0,1:T(8,128)S(1)} fusion(bf16[1,2048,2,704]{1,3,2,0:T(8,128)(2,1)S(1)} %bitcast.83, bf16[8,1,32,4,2048]{4,3,0,1,2:T(4,128)(2,1)S(1)} %all_to_all.10), kind=kOutput, calls=%fused_computation.13 | convolution fusion | flops 5905580032 | bytes 15728640 | tf_op jit(solution)/shard_map/tsecd,sdgf->tsecgf/dot_general | solution.py:24
  422.9 1.0 fusion.5
  423.9 2.4 copy.87
  426.3 3.7 convert_element_type.95
  430.0 6.3 %convert_bitcast_fusion = bf16[1024,1,2048]{2,0,1:T(8,128)(2,1)} fusion(bf16[1024,704]{1,0:T(8,128)(2,1)} %convert_element_type.95, bf16[1,704,2048]{2,1,0:T(8,128)(2,1)S(1)} %copy-done), kind=kOutput, calls=%fused_computation.8 | convolution fusion | flops 2954887168 | bytes 8519680 | tf_op jit(solution)/shard_map/bsf,sfd->bsd/dot_general | solution.py:125
  436.5 0.1 reshape.190
  436.8 0.1 mul.206
  437.0 0.1 mul.205
  437.2 37.1 %reduce-scatter.5.cloned.1.call-done = bf16[128,1,2048]{2,0,1:T(8,128)(2,1)} async-done(((bf16[1024,1,2048]{2,0,1:T(8,128)(2,1)}), bf16[128,1,2048]{2,0,1:T(8,128)(2,1)}) %reduce-scatter.5.cloned.1.call-update) | async-done | bytes 524304 | tf_op jit(solution)/shard_map/reduce_scatter | solution.py:124
  474.3 2.0 reshape.179
  476.3 9.8 %all-to-all-start.1 = ((bf16[32,4,1,2048]{3,1,2,0:T(4,128)(2,1)}), bf16[32,4,1,2048]{3,1,2,0:T(4,128)(2,1)}, u32[]{:S(2)}, u32[]{:S(2)}) async-start(bf16[32,4,1,2048]{3,1,2,0:T(4,128)(2,1)} %bitcast.81), calls=%async_computation.3 | async-start | bytes 1048576 | tf_op jit(solution)/shard_map/all_to_all | solution.py:133
  486.1 0.2 fusion.23
  486.4 1.0 gather_fusion.1
  487.4 0.1 reshape.193
  487.7 15.7 %all-to-all-done.1 = bf16[32,4,1,2048]{3,1,2,0:T(4,128)(2,1)} async-done(((bf16[32,4,1,2048]{3,1,2,0:T(4,128)(2,1)}), bf16[32,4,1,2048]{3,1,2,0:T(4,128)(2,1)}, u32[]{:S(2)}, u32[]{:S(2)}) %all-to-all-start.1) | async-done | bytes 524320 | tf_op jit(solution)/shard_map/all_to_all | solution.py:133
  503.4 1.2 reshape.180
  504.5 1.7 gather_fusion
  506.3 1.4 gather.11
  507.6 0.3 fusion.22
  508.0 1.2 multiply_reduce_fusion
  509.3 0.8 multiply_convert_fusion
  (59 shorter events, 1.1 us)
Async XLA Ops:
  7.2 422.9 %copy-start = (bf16[1,704,2048]{2,1,0:T(8,128)(2,1)S(1)}, bf16[1,704,2048]{2,1,0:T(8,128)(2,1)}, u32[]{:S(2)}) copy-start(bf16[1,704,2048]{2,1,0:T(8,128)(2,1)} %param.26) | copy-start | bytes 8650756
  7.2 5.7 %copy-start.5 = (f32[2048,2]{0,1:T(2,128)S(1)}, f32[2048,2]{0,1:T(2,128)}, u32[]{:S(2)}) copy-start(f32[2048,2]{0,1:T(2,128)} %param.17) | copy-start | bytes 49156
  7.2 6.1 %copy-start.4 = (s32[2048,2]{0,1:T(2,128)S(1)}, s32[2048,2]{0,1:T(2,128)}, u32[]{:S(2)}) copy-start(s32[2048,2]{0,1:T(2,128)} %param.16) | copy-start | bytes 49156
  7.2 256.7 %reduce-scatter.3.cloned.1.call-start = ((), (), s32[]{:S(2)}) async-start(), calls=%async_computation.4 | async-start | bytes 8650752 | tf_op jit(solution)/shard_map/reduce_scatter | solution.py:70
  14.7 14.3 %copy-start.11 = (bf16[8,64,2048]{2,1,0:T(8,128)(2,1)S(1)}, bf16[8,64,2048]{2,1,0:T(8,128)(2,1)}, u32[]{:S(2)}) copy-start(bf16[8,64,2048]{2,1,0:T(8,128)(2,1)} %param.18) | copy-start | bytes 6291460
  35.9 0.7 copy-start.7
  35.9 0.7 copy-start.3
  35.9 0.8 copy-start.6
  36.0 1.0 copy-start.9
  36.0 2.4 copy-start.10
  36.0 227.9 %copy-start.2 = (bf16[64,2048]{1,0:T(8,128)(2,1)S(1)}, bf16[64,2048]{1,0:T(8,128)(2,1)}, u32[]{:S(2)}) copy-start(bf16[64,2048]{1,0:T(8,128)(2,1)} %param.14) | copy-start | bytes 786436
  36.0 270.1 %all-gather.2.cloned.1.call-start = ((), (), s32[]{:S(2)}) async-start(), calls=%async_computation.5 | async-start | bytes 4718592 | tf_op jit(solution)/shard_map/all_gather | solution.py:120
  265.0 221.1 %copy-start.1 = (bf16[64,2048]{1,0:T(8,128)(2,1)}, bf16[64,2048]{1,0:T(8,128)(2,1)S(1)}, u32[]{:S(2)}) copy-start(bf16[64,2048]{1,0:T(8,128)(2,1)S(1)} %get-tuple-element.9) | copy-start | bytes 786436
  270.4 203.9 %reduce-scatter.5.cloned.1.call-start = ((), (), s32[]{:S(2)}) async-start(), calls=%async_computation.6 | async-start | bytes 4718592 | tf_op jit(solution)/shard_map/reduce_scatter | solution.py:124
  306.1 109.5 %slice-start = ((s8[5767168]{0:T(1024)(128)(4,1)}), s8[4194304]{0:T(1024)(128)(4,1)S(1)}, s32[]{:S(2)}) async-start(s8[5767168]{0:T(1024)(128)(4,1)} %bitcast.82), calls=%async_computation.7 | async-start | bytes 8388608
  311.7 103.9 %slice-start.1 = ((s8[5767168]{0:T(1024)(128)(4,1)}), s8[1572864]{0:T(1024)(128)(4,1)S(1)}, s32[]{:S(2)}) async-start(s8[5767168]{0:T(1024)(128)(4,1)} %bitcast.82), calls=%async_computation.8 | async-start | bytes 3145728
  436.4 0.8 copy-start.8
  436.4 49.7 %copy-start.12 = (bf16[2048,8]{0,1:T(8,128)(2,1)S(1)}, bf16[2048,8]{0,1:T(8,128)(2,1)}, u32[]{:S(2)}) copy-start(bf16[2048,8]{0,1:T(8,128)(2,1)} %param.20) | copy-start | bytes 98308
  476.3 27.1 %all-to-all-start.1 = ((bf16[32,4,1,2048]{3,1,2,0:T(4,128)(2,1)}), bf16[32,4,1,2048]{3,1,2,0:T(4,128)(2,1)}, u32[]{:S(2)}, u32[]{:S(2)}) async-start(bf16[32,4,1,2048]{3,1,2,0:T(4,128)(2,1)} %bitcast.81), calls=%async_computation.3 | async-start | bytes 1048576 | tf_op jit(solution)/shard_map/all_to_all | solution.py:133
Sparse Core Ops, SparseCore 0:
  36.1 227.6 reduce-scatter.2
  270.5 35.6 all-gather.1
  436.5 37.7 reduce-scatter.4
where the time goes:
time: 517 us
  waiting for transfers between devices  314 us (61%)
  blocking collectives  104 us (20%)
  matrix products  36.2 us (7%)
  local copies, waits for them, and re-layouts  32.7 us (6%)
  between operations  14.1 us (3%)
  starting transfers between devices  9.88 us (2%)
  other arithmetic  5.94 us (1%)
    reduce_scatter x1, waiting for transfers between devices, per_device(): lax.psum_scatter(jnp.dot(row_block, weight_flat, preferred_element_type=j...  225 us
    all_to_all x1, blocking collectives, per_device(): lax.all_to_all(collected, 'tensor', split_axis=2, concat_axis=2, tiled=True)  104 us
    reduce_scatter x1, waiting for transfers between devices, per_device(): lax.psum_scatter(jnp.einsum('bsf,sfd->bsd', row_block, w_down, preferred_...  37.1 us
    all_gather x1, waiting for transfers between devices, per_device(): collected = lax.all_gather(send_rows[None], 'expert', axis=0, tiled=True)  35.7 us
    all_to_all x1, waiting for transfers between devices, per_device(): lax.all_to_all(results, 'tensor', split_axis=0, concat_axis=0, tiled=True)  15.7 us
    dot_general x1, matrix products, per_device(): jnp.einsum('tke,tck->tec', weighted, context_part).astype(jnp.bfloat16)  14.3 us
  transfers between devices with their start and end apart: 4, of which 4 were waited for; matrix products, arithmetic and copies ran while one was open for 1% of the time, Pallas kernels for 0%

commit v1 on v0

--- a/solution.py
+++ b/solution.py
@@ -117,7 +117,10 @@
     )
     send_rows = jnp.dot(placer, normed, preferred_element_type=jnp.float32).astype(jnp.bfloat16)
     send_rows = send_rows.reshape(slots, n_tensor, capacity_rows, model_width)
-    collected = lax.all_gather(send_rows[None], "expert", axis=0, tiled=True)
+    collected = jnp.concatenate(
+        lax.all_to_all(jnp.stack([send_rows[None]] * lax.axis_size("expert")), "expert", 0, 0),
+        axis=0,
+    )
     arrived = lax.all_to_all(collected, "tensor", split_axis=2, concat_axis=2, tiled=True)
     hidden = activate(arrived, w_gate_up)
     row_block = hidden

time: 517 us -> 533 us (1.031)
  blocking collectives: 104 us -> 157 us
  waiting for transfers between devices: 314 us -> 278 us
    all_to_all x0 -> x1, blocking collectives: none -> 57.2 us  [per_device(): lax.all_to_all(jnp.stack([send_rows[None]] * lax.axis_size('expert')), 'e...]
    all_gather x1 -> x0, waiting for transfers between devices: 35.7 us -> none  [per_device(): collected = lax.all_gather(send_rows[None], 'expert', axis=0, tiled=True)]
    all_gather x1 -> x0, local copies, waits for them, and re-layouts: 5.57 us -> none  [per_device(): collected = lax.all_gather(send_rows[None], 'expert', axis=0, tiled=True)]
  transfers between devices with their start and end apart: 4 -> 3, of which waited for: 4 -> 3; matrix products, arithmetic and copies ran while one was open for 1% -> 1% of each run, Pallas kernels for 0% -> 0%
where the time goes in v1:
time: 533 us; the launch traced here: 532 us
  waiting for transfers between devices  278 us (52%)
  blocking collectives  157 us (29%)
  matrix products  36.3 us (7%)
  local copies, waits for them, and re-layouts  30.2 us (6%)
  between operations  14.4 us (3%)
  starting transfers between devices  9.82 us (2%)
  other arithmetic  6.73 us (1%)
    reduce_scatter x1, waiting for transfers between devices, per_device(): lax.psum_scatter(jnp.dot(row_block, weight_flat, preferred_element_type=j...  225 us
    all_to_all x1, blocking collectives, per_device(): lax.all_to_all(collected, 'tensor', split_axis=2, concat_axis=2, tiled=True)  99.9 us
    all_to_all x1, blocking collectives, per_device(): lax.all_to_all(jnp.stack([send_rows[None]] * lax.axis_size('expert')), 'e...  57.2 us
    reduce_scatter x1, waiting for transfers between devices, per_device(): lax.psum_scatter(jnp.einsum('bsf,sfd->bsd', row_block, w_down, preferred_...  37.6 us
    all_to_all x1, waiting for transfers between devices, per_device(): lax.all_to_all(results, 'tensor', split_axis=0, concat_axis=0, tiled=True)  15.7 us
    dot_general x1, matrix products, per_device(): jnp.einsum('tke,tck->tec', weighted, context_part).astype(jnp.bfloat16)  14.3 us
  transfers between devices with their start and end apart: 3, of which 3 were waited for; matrix products, arithmetic and copies ran while one was open for 1% of the time, Pallas kernels for 0%

profile of v1, /device:TPU:7, one launch (start us, length us, event | category | flops | bytes accessed | tf_op | source)
XLA Modules:
  0.0 532.3 jit_solution(17688067235365034659)
XLA Ops:
  7.2 2.2 copy.77
  9.4 1.4 reshape.182
  10.8 2.1 copy.78
  12.9 0.8 broadcast_subtract_fusion
  13.8 0.3 copy.76
  14.1 1.4 copy.75
  15.5 14.3 %convolution_convert_fusion = bf16[2048,8,64]{2,1,0:T(8,128)(2,1)S(1)} fusion(bf16[2048,64,2]{1,2,0:T(2,128)(2,1)} %copy.78, bf16[2048,2]{1,0:T(8,128)(2,1)S(1)} %copy.76, s32[2048,2]{1,0:T(8,128)} %copy.75), kind=kOutput, calls=%fused_computation.14 | convolution fusion | flops 4259840 | bytes 2646016 | tf_op jit(solution)/shard_map/tke,tck->tec/dot_general | solution.py:64
  29.8 7.0 %bitcast_convert_fusion = bf16[2048,2048]{1,0:T(8,128)(2,1)} fusion(bf16[8,64,2048]{2,1,0:T(8,128)(2,1)S(1)} %copy-done.10, bf16[2048,8,64]{2,1,0:T(8,128)(2,1)S(1)} %convolution_convert_fusion), kind=kOutput, calls=%fused_computation.2 | convolution fusion | flops 4299161600 | bytes 12582912 | tf_op jit(solution)/shard_map/dot_general | solution.py:71
  36.9 0.6 copy-done.6
  37.5 0.1 convert_reduce_fusion.1
  37.7 0.1 and_select_fusion.1
  38.0 0.1 eq.133
  38.1 0.1 eq.119
  38.3 0.2 convert_reduce_fusion
  38.6 0.2 reduce_window_sum.11
  38.7 0.2 select_reduce_fusion
  38.9 0.1 reduce_sum.92
  39.1 0.1 select_reduce_fusion.2
  39.3 224.6 %reduce-scatter.3.cloned.1.call-done = bf16[64,2048]{1,0:T(8,128)(2,1)} async-done(((bf16[2048,2048]{1,0:T(8,128)(2,1)}), bf16[64,2048]{1,0:T(8,128)(2,1)}) %reduce-scatter.3.cloned.1.call-update) | async-done | bytes 262160 | tf_op jit(solution)/shard_map/reduce_scatter | solution.py:70
  264.0 1.1 fusion.16
  265.1 1.1 convolution_convert_fusion.1
  266.3 2.0 stack_broadcast_in_dim_reshape.2
  268.3 1.3 copy.84
  269.7 0.5 stack.12
  270.2 57.2 %all_to_all.15 = bf16[8,1,1,32,4,2048]{5,3,4,2,1,0:T(8,128)(2,1)S(1)} all-to-all(bf16[8,1,1,32,4,2048]{5,3,4,2,1,0:T(8,128)(2,1)S(1)} %stack.12), channel_id=1, replica_groups=mesh['expert'=8,'tensor'=32] {'expert'}, dimensions={0} | all-to-all | bytes 8388608 | tf_op jit(solution)/shard_map/all_to_all | solution.py:121
  327.4 3.2 copy.85
  330.6 99.9 %all_to_all.16 = bf16[8,1,32,4,2048]{4,3,0,1,2:T(4,128)(2,1)S(1)} all-to-all(bf16[8,1,32,4,2048]{4,3,0,1,2:T(4,128)(2,1)S(1)} %copy.85), channel_id=1, replica_groups=mesh['expert'=8,'tensor'=32] {'tensor'}, dimensions={2} | all-to-all | bytes 8388608 | tf_op jit(solution)/shard_map/all_to_all | solution.py:124
  430.5 7.3 %fusion.7 = f32[8,1,32,4,2,704]{5,2,4,3,0,1:T(8,128)S(1)} fusion(bf16[1,2048,2,704]{1,3,2,0:T(8,128)(2,1)S(1)} %bitcast.85, bf16[8,1,32,4,2048]{4,3,0,1,2:T(4,128)(2,1)S(1)} %all_to_all.16), kind=kOutput, calls=%fused_computation.13 | convolution fusion | flops 5905580032 | bytes 15728640 | tf_op jit(solution)/shard_map/tsecd,sdgf->tsecgf/dot_general | solution.py:24
  437.8 1.0 fusion.5
  438.8 2.4 copy.87
  441.2 3.7 convert_element_type.95
  444.9 6.4 %convert_bitcast_fusion = bf16[1024,1,2048]{2,0,1:T(8,128)(2,1)} fusion(bf16[1024,704]{1,0:T(8,128)(2,1)} %convert_element_type.95, bf16[1,704,2048]{2,1,0:T(8,128)(2,1)S(1)} %copy-done), kind=kOutput, calls=%fused_computation.8 | convolution fusion | flops 2954887168 | bytes 8519680 | tf_op jit(solution)/shard_map/bsf,sfd->bsd/dot_general | solution.py:128
  451.4 0.1 reshape.198
  451.6 0.1 mul.206
  451.9 0.1 mul.205
  452.1 37.6 %reduce-scatter.5.cloned.1.call-done = bf16[128,1,2048]{2,0,1:T(8,128)(2,1)} async-done(((bf16[1024,1,2048]{2,0,1:T(8,128)(2,1)}), bf16[128,1,2048]{2,0,1:T(8,128)(2,1)}) %reduce-scatter.5.cloned.1.call-update) | async-done | bytes 524304 | tf_op jit(solution)/shard_map/reduce_scatter | solution.py:127
  489.7 2.0 reshape.187
  491.7 9.7 %all-to-all-start.2 = ((bf16[32,4,1,2048]{3,1,2,0:T(4,128)(2,1)}), bf16[32,4,1,2048]{3,1,2,0:T(4,128)(2,1)}, u32[]{:S(2)}, u32[]{:S(2)}) async-start(bf16[32,4,1,2048]{3,1,2,0:T(4,128)(2,1)} %bitcast.83), calls=%async_computation.4 | async-start | bytes 1048576 | tf_op jit(solution)/shard_map/all_to_all | solution.py:136
  501.5 0.2 fusion.23
  501.7 1.0 gather_fusion.1
  502.8 0.1 reshape.201
  503.0 15.7 %all-to-all-done.2 = bf16[32,4,1,2048]{3,1,2,0:T(4,128)(2,1)} async-done(((bf16[32,4,1,2048]{3,1,2,0:T(4,128)(2,1)}), bf16[32,4,1,2048]{3,1,2,0:T(4,128)(2,1)}, u32[]{:S(2)}, u32[]{:S(2)}) %all-to-all-start.2) | async-done | bytes 524320 | tf_op jit(solution)/shard_map/all_to_all | solution.py:136
  518.8 1.2 reshape.188
  519.9 1.7 gather_fusion
  521.7 1.4 gather.11
  523.0 0.3 fusion.22
  523.4 1.2 multiply_reduce_fusion
  524.7 0.8 multiply_convert_fusion
  (56 shorter events, 1.2 us)
Async XLA Ops:
  7.2 437.7 %copy-start = (bf16[1,704,2048]{2,1,0:T(8,128)(2,1)S(1)}, bf16[1,704,2048]{2,1,0:T(8,128)(2,1)}, u32[]{:S(2)}) copy-start(bf16[1,704,2048]{2,1,0:T(8,128)(2,1)} %param.26) | copy-start | bytes 8650756
  7.2 6.9 %copy-start.4 = (s32[2048,2]{0,1:T(2,128)S(1)}, s32[2048,2]{0,1:T(2,128)}, u32[]{:S(2)}) copy-start(s32[2048,2]{0,1:T(2,128)} %param.16) | copy-start | bytes 49156
  7.2 256.8 %reduce-scatter.3.cloned.1.call-start = ((), (), s32[]{:S(2)}) async-start(), calls=%async_computation.5 | async-start | bytes 8650752 | tf_op jit(solution)/shard_map/reduce_scatter | solution.py:70
  15.5 14.3 %copy-start.10 = (bf16[8,64,2048]{2,1,0:T(8,128)(2,1)S(1)}, bf16[8,64,2048]{2,1,0:T(8,128)(2,1)}, u32[]{:S(2)}) copy-start(bf16[8,64,2048]{2,1,0:T(8,128)(2,1)} %param.18) | copy-start | bytes 6291460
  36.7 0.7 copy-start.6
  36.8 0.7 copy-start.3
  36.8 0.8 copy-start.5
  36.8 1.0 copy-start.8
  36.8 2.4 copy-start.9
  36.8 227.2 %copy-start.2 = (bf16[64,2048]{1,0:T(8,128)(2,1)S(1)}, bf16[64,2048]{1,0:T(8,128)(2,1)}, u32[]{:S(2)}) copy-start(bf16[64,2048]{1,0:T(8,128)(2,1)} %param.14) | copy-start | bytes 786436
  36.8 452.9 %reduce-scatter.5.cloned.1.call-start = ((), (), s32[]{:S(2)}) async-start(), calls=%async_computation.6 | async-start | bytes 4718592 | tf_op jit(solution)/shard_map/reduce_scatter | solution.py:127
  265.1 236.4 %copy-start.1 = (bf16[64,2048]{1,0:T(8,128)(2,1)}, bf16[64,2048]{1,0:T(8,128)(2,1)S(1)}, u32[]{:S(2)}) copy-start(bf16[64,2048]{1,0:T(8,128)(2,1)S(1)} %get-tuple-element.9) | copy-start | bytes 786436
  327.4 103.1 %slice-start = ((s8[5767168]{0:T(1024)(128)(4,1)}), s8[4194304]{0:T(1024)(128)(4,1)S(1)}, s32[]{:S(2)}) async-start(s8[5767168]{0:T(1024)(128)(4,1)} %bitcast.84), calls=%async_computation.7 | async-start | bytes 8388608
  330.6 99.9 %slice-start.1 = ((s8[5767168]{0:T(1024)(128)(4,1)}), s8[1572864]{0:T(1024)(128)(4,1)S(1)}, s32[]{:S(2)}) async-start(s8[5767168]{0:T(1024)(128)(4,1)} %bitcast.84), calls=%async_computation.8 | async-start | bytes 3145728
  451.3 0.8 copy-start.7
  451.3 50.2 %copy-start.11 = (bf16[2048,8]{0,1:T(8,128)(2,1)S(1)}, bf16[2048,8]{0,1:T(8,128)(2,1)}, u32[]{:S(2)}) copy-start(bf16[2048,8]{0,1:T(8,128)(2,1)} %param.20) | copy-start | bytes 98308
  491.7 27.1 %all-to-all-start.2 = ((bf16[32,4,1,2048]{3,1,2,0:T(4,128)(2,1)}), bf16[32,4,1,2048]{3,1,2,0:T(4,128)(2,1)}, u32[]{:S(2)}, u32[]{:S(2)}) async-start(bf16[32,4,1,2048]{3,1,2,0:T(4,128)(2,1)} %bitcast.83), calls=%async_computation.4 | async-start | bytes 1048576 | tf_op jit(solution)/shard_map/all_to_all | solution.py:136
Sparse Core Ops, SparseCore 0:
  36.9 226.9 reduce-scatter.2
  451.4 38.2 reduce-scatter.4
